TPU v7x, 32 devices: a whole 2x2x4 slice. The times are simulated.
32 devices in a mesh: ctx: 8 (over y, x, core), fsdp: 4 (over z).
Axes of the slice: x: 2, y: 2, z: 4, core: 2. Of those that a mesh axis runs over, the one named last changes fastest.
Arguments:
- hidden_in: float32 [4, 1024, 2048], P('fsdp', 'ctx'), may hold values from -6 to 6
- block_map: int32 [16], replicated, may hold values from 0 to 15, each once
- doc_ids: int32 [4, 1024], P('fsdp'), may hold values from 0 to 3, never falling along the last dimension, each value on 1 to 512 neighbouring positions
- routes: int32 [4, 1024, 8], P('fsdp', 'ctx'), may hold values from 0 to 15, all different within a row; in each aligned block of 128 rows (0 to 127, 128 to 255, ..., all dimensions but the last counted through in order) at most 96 rows name the same one
- attn_gain: float32 [2048], replicated, may hold values from 0.5 to 1.5
- query_proj: bfloat16 [2048, 4096], P('fsdp'), may hold values from -0.125 to 0.125
- key_proj: bfloat16 [2048, 512], P('fsdp'), may hold values from -0.125 to 0.125
- value_proj: bfloat16 [2048, 512], P('fsdp'), may hold values from -0.125 to 0.125
- query_gain: float32 [128], replicated, may hold values from 0.1 to 1.9
- key_gain: float32 [128], replicated, may hold values from 0.1 to 1.9
- out_proj: bfloat16 [4096, 2048], P('fsdp'), may hold values from -0.375 to 0.375
- ffn_gain: float32 [2048], replicated, may hold values from 0.5 to 1.5
- router_proj: bfloat16 [2048, 16], P('fsdp'), may hold values from -0.125 to 0.125
- expert_gate: bfloat16 [16, 2048, 768], P('ctx', 'fsdp'), may hold values from -0.125 to 0.125
- expert_up: bfloat16 [16, 2048, 768], P('ctx', 'fsdp'), may hold values from -0.125 to 0.125
- expert_down: bfloat16 [16, 768, 2048], P('ctx', 'fsdp'), may hold values from -0.4375 to 0.4375
- cotangent: float32 [4, 1024, 2048], P('fsdp', 'ctx'), may hold values from -6 to 6
Outputs:
- layer_out: float32 [4, 1024, 2048], P('fsdp', 'ctx')
- input_grad: float32 [4, 1024, 2048], P('fsdp', 'ctx')
- attn_gain_grad: float32 [2048], replicated
- query_proj_grad: float32 [2048, 4096], P('fsdp')
- key_proj_grad: float32 [2048, 512], P('fsdp')
- value_proj_grad: float32 [2048, 512], P('fsdp')
- query_gain_grad: float32 [128], replicated
- key_gain_grad: float32 [128], replicated
- out_proj_grad: float32 [4096, 2048], P('fsdp')
- ffn_gain_grad: float32 [2048], replicated
- router_grad: float32 [2048, 16], P('fsdp')
- gate_grad: float32 [16, 2048, 768], P('ctx', 'fsdp')
- up_grad: float32 [16, 2048, 768], P('ctx', 'fsdp')
- down_grad: float32 [16, 768, 2048], P('ctx', 'fsdp')
Inputs may be any that keep to these rules, and one draw needn't show every extreme that they name: `block_map`: A permutation: every block of positions is held by exactly one stored block. `doc_ids`: along the positions of a sequence the document numbers never fall; each document is 1 to 512 positions long and one is exactly that long. `routes`: each token names 8 different experts. Within the 128 stored rows of one device (aligned blocks of rows), no expert is named by more than 96 of them, and in every draw some expert is named by exactly 96.
All inputs are finite; a program needn't handle non-finite values.
Results may differ from a plain program's by a relative error of at most 0.024.
Values may be sent and summed in bfloat16 or wider, within the bound.
No kernel may reach another device: no remote copies, remote signals or barrier semaphores. Data moves between devices by JAX's collectives and lax.ppermute only.
A program may use at most 320 MiB of HBM per device.

v0:
```python
import jax
import jax.numpy as jnp
from jax import lax
from jax.sharding import PartitionSpec as P

D = 2048
HEADS = 32
KV_HEADS = 4
HEAD_DIM = 128
TOP = 8
EPSILON = 1e-06
ROPE_BASE = 1000000.0
NEG_FILL = -1e30


def matmul(left, right):
    return jnp.dot(left, right, preferred_element_type=jnp.float32)


def contract(form, left, right):
    return jnp.einsum(form, left, right, preferred_element_type=jnp.float32)


def rms_scale(field):
    return lax.rsqrt(jnp.mean(field * field, axis=-1, keepdims=True) + EPSILON)


def rotary(positions):
    halfway = HEAD_DIM // 2
    inverse = ROPE_BASE ** (-2.0 * jnp.arange(halfway, dtype=jnp.float32) / HEAD_DIM)
    angle = positions.astype(jnp.float32)[:, None] * inverse[None, :]
    return (jnp.cos(angle), jnp.sin(angle))


def rotate(field, cosine, sine_table):
    halfway = field.shape[-1] // 2
    former = field[..., :halfway]
    latter = field[..., halfway:]
    cos_b = cosine[:, None, :]
    sin_b = sine_table[:, None, :]
    return jnp.concatenate(
        [former * cos_b - latter * sin_b, latter * cos_b + former * sin_b], axis=-1
    )


def rotate_back(field, cosine, sine_table):
    halfway = field.shape[-1] // 2
    former = field[..., :halfway]
    latter = field[..., halfway:]
    cos_b = cosine[:, None, :]
    sin_b = sine_table[:, None, :]
    return jnp.concatenate(
        [former * cos_b + latter * sin_b, latter * cos_b - former * sin_b], axis=-1
    )


def norm_back(grad, normed, inv_scale, factor):
    lead_axes = tuple(range(grad.ndim - 1))
    factor_grad = jnp.sum(grad * normed, axis=lead_axes)
    scaled = grad * factor
    return (
        inv_scale * (scaled - normed * jnp.mean(scaled * normed, axis=-1, keepdims=True)),
        factor_grad,
    )


def per_device(
    hidden_in,
    block_map,
    doc_ids,
    routes,
    attn_gain,
    query_proj,
    key_proj,
    value_proj,
    query_gain,
    key_gain,
    out_proj,
    ffn_gain,
    router_proj,
    expert_gate,
    expert_up,
    expert_down,
    cotangent,
):
    tokens = hidden_in.shape[1]
    ctx_size = lax.axis_size("ctx")
    local_experts = expert_gate.shape[0]
    experts = local_experts * ctx_size
    capacity = min(tokens, 3 * tokens * TOP // (2 * experts))
    block_len = tokens // 2
    group_size = HEADS // KV_HEADS
    score_scale = HEAD_DIM ** (-0.5)
    ctx_index = lax.axis_index("ctx")
    own_blocks = lax.dynamic_slice_in_dim(block_map, 2 * ctx_index, 2, 0)
    offsets = jnp.arange(block_len, dtype=jnp.int32)
    local_pos = (own_blocks[:, None] * block_len + offsets[None, :]).reshape(-1)
    all_pos = (block_map[:, None] * block_len + offsets[None, :]).reshape(-1)
    doc_row = doc_ids[0]
    same_doc = jnp.take(doc_row, all_pos)[None, :] == jnp.take(doc_row, local_pos)[:, None]
    visible = (all_pos[None, :] <= local_pos[:, None]) & same_doc
    cosine, sine_table = rotary(local_pos)
    hidden = hidden_in[0]
    first_scale = rms_scale(hidden)
    first_normed = hidden * first_scale
    first_input = (first_normed * attn_gain).astype(jnp.bfloat16)
    w_query, w_key, w_value, w_out = (
        lax.all_gather(query_proj, "fsdp", axis=0, tiled=True),
        lax.all_gather(key_proj, "fsdp", axis=0, tiled=True),
        lax.all_gather(value_proj, "fsdp", axis=0, tiled=True),
        lax.all_gather(out_proj, "fsdp", axis=0, tiled=True),
    )
    query_raw = matmul(first_input, w_query).reshape(tokens, HEADS, HEAD_DIM)
    key_raw = matmul(first_input, w_key).reshape(tokens, KV_HEADS, HEAD_DIM)
    value_low = matmul(first_input, w_value).astype(jnp.bfloat16)
    query_scale = rms_scale(query_raw)
    query_normed = query_raw * query_scale
    query_rot = rotate(query_normed * query_gain, cosine, sine_table).astype(jnp.bfloat16)
    key_scale = rms_scale(key_raw)
    key_normed = key_raw * key_scale
    key_rot = (
        rotate(key_normed * key_gain, cosine, sine_table)
        .reshape(tokens, KV_HEADS * HEAD_DIM)
        .astype(jnp.bfloat16)
    )
    keys_all, values_all = (
        lax.all_gather(key_rot, "ctx", axis=0, tiled=True),
        lax.all_gather(value_low, "ctx", axis=0, tiled=True),
    )

    def split_keys(flat):
        return flat.reshape(-1, KV_HEADS, HEAD_DIM).transpose(1, 0, 2)

    def join_keys(stacked):
        return stacked.transpose(1, 0, 2).reshape(-1, KV_HEADS * HEAD_DIM)

    def split_queries(flat):
        return flat.reshape(tokens, KV_HEADS, group_size, HEAD_DIM).transpose(1, 2, 0, 3)

    def join_queries(stacked):
        return stacked.transpose(2, 0, 1, 3).reshape(tokens, HEADS * HEAD_DIM)

    def masked_scores(q_block, k_block):
        scores = contract("gtd,sd->gts", q_block, k_block) * score_scale
        return jnp.where(visible[None], scores, NEG_FILL)

    def head_forward(items):
        q_block, k_block, v_block = items
        scores = masked_scores(q_block, k_block)
        peak = jnp.max(scores, axis=-1, keepdims=True)
        expo = jnp.exp(scores - peak)
        total = jnp.sum(expo, axis=-1, keepdims=True)
        probs = (expo / total).astype(jnp.bfloat16)
        mixed = contract("gts,sd->gtd", probs, v_block)
        return (mixed, (peak + jnp.log(total))[..., 0])

    query_groups = split_queries(query_rot)
    attn_out, log_sums = lax.map(
        head_forward, (query_groups, split_keys(keys_all), split_keys(values_all))
    )
    attended = join_queries(attn_out).astype(jnp.bfloat16)
    middle = hidden + matmul(attended, w_out)
    second_scale = rms_scale(middle)
    second_normed = middle * second_scale
    second_input = (second_normed * ffn_gain).astype(jnp.bfloat16)
    w_gate, w_up, w_down, w_router = (
        lax.all_gather(expert_gate, "fsdp", axis=1, tiled=True),
        lax.all_gather(expert_up, "fsdp", axis=1, tiled=True),
        lax.all_gather(expert_down, "fsdp", axis=1, tiled=True),
        lax.all_gather(router_proj, "fsdp", axis=0, tiled=True),
    )
    logits = matmul(second_input, w_router)
    route_ids = routes[0]
    chosen = jnp.take_along_axis(logits, route_ids, axis=1)
    route_weights = jax.nn.softmax(chosen, axis=-1)
    flat_ids = route_ids.reshape(-1)
    expert_range = jnp.arange(experts, dtype=jnp.int32)
    one_hot = (flat_ids[:, None] == expert_range[None, :]).astype(jnp.int32)
    earlier = jnp.cumsum(one_hot, axis=0) - one_hot
    slot_index = jnp.sum(earlier * one_hot, axis=1)
    target = flat_ids * capacity + slot_index

    def dispatch(route_rows):
        buffer = jnp.zeros((experts * capacity, D), jnp.bfloat16).at[target].set(route_rows)
        return buffer.reshape(ctx_size, local_experts, capacity, D)

    def collect(returned):
        return jnp.take(returned.reshape(experts * capacity, D), target, axis=0)

    received = lax.all_to_all(
        dispatch(jnp.repeat(second_input, TOP, axis=0)),
        "ctx",
        split_axis=0,
        concat_axis=2,
        tiled=True,
    )[0]
    gate_val = contract("erd,edf->erf", received, w_gate)
    up_val = contract("erd,edf->erf", received, w_up)
    gate_sig = jax.nn.sigmoid(gate_val)
    hid_low = (gate_val * gate_sig * up_val).astype(jnp.bfloat16)
    expert_out = contract("erf,efd->erd", hid_low, w_down).astype(jnp.bfloat16)
    route_out = (
        collect(lax.all_to_all(expert_out[None], "ctx", split_axis=2, concat_axis=0, tiled=True))
        .reshape(tokens, TOP, D)
        .astype(jnp.float32)
    )
    layer_out = middle + jnp.einsum("tr,trd->td", route_weights, route_out)
    grad_out = cotangent[0]
    grad_weights = jnp.einsum("td,trd->tr", grad_out, route_out)
    grad_routes = (
        (route_weights[:, :, None] * grad_out[:, None, :])
        .astype(jnp.bfloat16)
        .reshape(tokens * TOP, D)
    )
    grad_expert = lax.all_to_all(
        dispatch(grad_routes), "ctx", split_axis=0, concat_axis=2, tiled=True
    )[0]
    grad_hid = contract("erd,efd->erf", grad_expert, w_down)
    down_grad_full = contract("erf,erd->efd", hid_low, grad_expert)
    grad_gate = (grad_hid * up_val * gate_sig * (1.0 + gate_val * (1.0 - gate_sig))).astype(
        jnp.bfloat16
    )
    grad_up = (grad_hid * gate_val * gate_sig).astype(jnp.bfloat16)
    gate_grad_full = contract("erd,erf->edf", received, grad_gate)
    up_grad_full = contract("erd,erf->edf", received, grad_up)
    grad_rows = (
        contract("erf,edf->erd", grad_gate, w_gate) + contract("erf,edf->erd", grad_up, w_up)
    ).astype(jnp.bfloat16)
    grad_copies = collect(
        lax.all_to_all(grad_rows[None], "ctx", split_axis=2, concat_axis=0, tiled=True)
    ).reshape(tokens, TOP, D)
    grad_chosen = route_weights * (
        grad_weights - jnp.sum(route_weights * grad_weights, axis=-1, keepdims=True)
    )
    route_hot = (route_ids[:, :, None] == expert_range[None, None, :]).astype(jnp.float32)
    grad_logits = jnp.einsum("tr,tre->te", grad_chosen, route_hot).astype(jnp.bfloat16)
    router_grad_full = contract("td,te->de", second_input, grad_logits)
    grad_second = jnp.sum(grad_copies.astype(jnp.float32), axis=1) + contract(
        "te,de->td", grad_logits, w_router
    )
    grad_middle, ffn_gain_grad = norm_back(grad_second, second_normed, second_scale, ffn_gain)
    grad_middle = grad_middle + grad_out
    w_query, w_key, w_value, w_out = (
        lax.all_gather(query_proj, "fsdp", axis=0, tiled=True),
        lax.all_gather(key_proj, "fsdp", axis=0, tiled=True),
        lax.all_gather(value_proj, "fsdp", axis=0, tiled=True),
        lax.all_gather(out_proj, "fsdp", axis=0, tiled=True),
    )
    keys_all, values_all = (
        lax.all_gather(key_rot, "ctx", axis=0, tiled=True),
        lax.all_gather(value_low, "ctx", axis=0, tiled=True),
    )
    grad_branch = grad_middle.astype(jnp.bfloat16)
    out_grad_full = contract("tq,td->qd", attended, grad_branch)
    grad_attended = contract("td,qd->tq", grad_branch, w_out).astype(jnp.bfloat16)

    def head_backward(items):
        q_block, k_block, v_block, g_block, lse_block = items
        probs = jnp.exp(masked_scores(q_block, k_block) - lse_block[..., None])
        grad_probs = contract("gtd,sd->gts", g_block, v_block)
        delta = jnp.sum(probs * grad_probs, axis=-1, keepdims=True)
        grad_scores = (probs * (grad_probs - delta)).astype(jnp.bfloat16)
        grad_q = contract("gts,sd->gtd", grad_scores, k_block) * score_scale
        grad_k = contract("gts,gtd->sd", grad_scores, q_block) * score_scale
        grad_v = contract("gts,gtd->sd", probs.astype(jnp.bfloat16), g_block)
        return (grad_q, grad_k, grad_v)

    grad_qgroups, grad_kheads, grad_vheads = lax.map(
        head_backward,
        (
            query_groups,
            split_keys(keys_all),
            split_keys(values_all),
            split_queries(grad_attended),
            log_sums,
        ),
    )
    grad_key_rot, grad_value = (
        lax.psum_scatter(
            join_keys(grad_kheads).astype(jnp.bfloat16), "ctx", scatter_dimension=0, tiled=True
        ).astype(jnp.float32),
        lax.psum_scatter(
            join_keys(grad_vheads).astype(jnp.bfloat16), "ctx", scatter_dimension=0, tiled=True
        ).astype(jnp.float32),
    )
    grad_query_rot = join_queries(grad_qgroups).reshape(tokens, HEADS, HEAD_DIM)
    grad_query, query_gain_grad = norm_back(
        rotate_back(grad_query_rot, cosine, sine_table), query_normed, query_scale, query_gain
    )
    grad_key, key_gain_grad = norm_back(
        rotate_back(grad_key_rot.reshape(tokens, KV_HEADS, HEAD_DIM), cosine, sine_table),
        key_normed,
        key_scale,
        key_gain,
    )
    grad_query = grad_query.reshape(tokens, HEADS * HEAD_DIM).astype(jnp.bfloat16)
    grad_key = grad_key.reshape(tokens, KV_HEADS * HEAD_DIM).astype(jnp.bfloat16)
    grad_value = grad_value.astype(jnp.bfloat16)
    query_grad_full = contract("td,tq->dq", first_input, grad_query)
    key_grad_full = contract("td,tq->dq", first_input, grad_key)
    value_grad_full = contract("td,tq->dq", first_input, grad_value)
    grad_first = (
        contract("tq,dq->td", grad_query, w_query)
        + contract("tq,dq->td", grad_key, w_key)
        + contract("tq,dq->td", grad_value, w_value)
    )
    grad_hidden, attn_gain_grad = norm_back(grad_first, first_normed, first_scale, attn_gain)
    grad_hidden = grad_hidden + grad_middle
    gate_grad, up_grad, down_grad = (
        lax.psum_scatter(
            gate_grad_full.astype(jnp.bfloat16), "fsdp", scatter_dimension=1, tiled=True
        ).astype(jnp.float32),
        lax.psum_scatter(
            up_grad_full.astype(jnp.bfloat16), "fsdp", scatter_dimension=1, tiled=True
        ).astype(jnp.float32),
        lax.psum_scatter(
            down_grad_full.astype(jnp.bfloat16), "fsdp", scatter_dimension=1, tiled=True
        ).astype(jnp.float32),
    )
    shard_grads = (
        lax.psum_scatter(
            query_grad_full.astype(jnp.bfloat16), "fsdp", scatter_dimension=0, tiled=True
        ).astype(jnp.float32),
        lax.psum_scatter(
            key_grad_full.astype(jnp.bfloat16), "fsdp", scatter_dimension=0, tiled=True
        ).astype(jnp.float32),
        lax.psum_scatter(
            value_grad_full.astype(jnp.bfloat16), "fsdp", scatter_dimension=0, tiled=True
        ).astype(jnp.float32),
        lax.psum_scatter(
            out_grad_full.astype(jnp.bfloat16), "fsdp", scatter_dimension=0, tiled=True
        ).astype(jnp.float32),
        lax.psum_scatter(
            router_grad_full.astype(jnp.bfloat16), "fsdp", scatter_dimension=0, tiled=True
        ).astype(jnp.float32),
    )
    query_grad, key_grad, value_grad, out_grad, router_grad = (
        lax.psum(shard_grads[0].astype(jnp.bfloat16), "ctx").astype(jnp.float32),
        lax.psum(shard_grads[1].astype(jnp.bfloat16), "ctx").astype(jnp.float32),
        lax.psum(shard_grads[2].astype(jnp.bfloat16), "ctx").astype(jnp.float32),
        lax.psum(shard_grads[3].astype(jnp.bfloat16), "ctx").astype(jnp.float32),
        lax.psum(shard_grads[4].astype(jnp.bfloat16), "ctx").astype(jnp.float32),
    )
    attn_gain_total, query_gain_total, key_gain_total, ffn_gain_total = lax.psum(
        (attn_gain_grad, query_gain_grad, key_gain_grad, ffn_gain_grad), ("ctx", "fsdp")
    )
    return (
        layer_out[None],
        grad_hidden[None],
        attn_gain_total,
        query_grad,
        key_grad,
        value_grad,
        query_gain_total,
        key_gain_total,
        out_grad,
        ffn_gain_total,
        router_grad,
        gate_grad,
        up_grad,
        down_grad,
    )


def solution(mesh):
    placed = (
        P("fsdp", "ctx", None),
        P(),
        P("fsdp", None),
        P("fsdp", "ctx", None),
        P(),
        P("fsdp", None),
        P("fsdp", None),
        P("fsdp", None),
        P(),
        P(),
        P("fsdp", None),
        P(),
        P("fsdp", None),
        P("ctx", "fsdp", None),
        P("ctx", "fsdp", None),
        P("ctx", "fsdp", None),
        P("fsdp", "ctx", None),
    )
    return jax.shard_map(
        per_device,
        mesh=mesh,
        in_specs=placed,
        out_specs=(
            P("fsdp", "ctx", None),
            P("fsdp", "ctx", None),
            P(),
            P("fsdp", None),
            P("fsdp", None),
            P("fsdp", None),
            P(),
            P(),
            P("fsdp", None),
            P(),
            P("fsdp", None),
            P("ctx", "fsdp", None),
            P("ctx", "fsdp", None),
            P("ctx", "fsdp", None),
        ),
        check_vma=False,
    )
```

profile of v0, /device:TPU:0, one launch (start us, length us, event | category | flops | bytes accessed | tf_op | source)
XLA Modules:
  0.0 2629.6 jit_solution(3409406196270798106)
XLA Ops:
  14.3 43.7 %all-gather.12.cloned.1.call-done = bf16[2048,512]{1,0:T(8,128)(2,1)} async-done(((bf16[512,512]{1,0:T(8,128)(2,1)}), bf16[2048,512]{1,0:T(8,128)(2,1)}) %all-gather.12.cloned.1.call-update) | async-done | bytes 2097168 | tf_op jit(solution)/shard_map/all_gather | solution.py:109
  65.3 38.8 %all-gather.16.cloned.1.call-done = bf16[2048,512]{1,0:T(8,128)(2,1)} async-done(((bf16[512,512]{1,0:T(8,128)(2,1)}), bf16[2048,512]{1,0:T(8,128)(2,1)}) %all-gather.16.cloned.1.call-update) | async-done | bytes 2097168 | tf_op jit(solution)/shard_map/all_gather | solution.py:110
  110.2 4.5 gather_fusion
  114.7 13.6 all_gather.42
  128.5 4.5 reduce-window.6
  135.4 19.2 all-gather.18.cloned.1.call-done
  157.0 285.8 %all-gather.10.cloned.1.call-done = bf16[2048,4096]{1,0:T(8,128)(2,1)} async-done(((bf16[512,4096]{1,0:T(8,128)(2,1)}), bf16[2048,4096]{1,0:T(8,128)(2,1)}) %all-gather.10.cloned.1.call-update) | async-done | bytes 16777232 | tf_op jit(solution)/shard_map/all_gather | solution.py:108
  442.8 23.1 copy.78
  465.9 8.3 multiply_reduce_fusion.3
  481.0 27.0 %while.28 = (s32[]{:T(128)}, bf16[4,8,128,128]{2,3,1,0:T(8,128)(2,1)}, f32[4,8,128]{2,1,0:T(8,128)}, bf16[4,8,128,128]{3,2,1,0:T(8,128)(2,1)S(1)}, bf16[4,1024,1...) while((s32[]{:T(128)}, ...), condition=%wide.region_6.7_spmd.clone, body=%wide.region_3.6_spmd.clone.sunk | while | flops 549846016 | bytes 14462573 | solution.py:158
  508.1 221.2 %all-gather.20.cloned.1.call-done = bf16[4096,2048]{1,0:T(8,128)(2,1)} async-done(((bf16[1024,2048]{1,0:T(8,128)(2,1)}), bf16[4096,2048]{1,0:T(8,128)(2,1)}) %all-gather.20.cloned.1.call-update) | async-done | bytes 16777232 | tf_op jit(solution)/shard_map/all_gather | solution.py:111
  729.2 8.6 multiply_reduce_fusion.8
  739.2 7.2 gather_fusion.2
  747.2 10.7 scatter_custom_fusion.1
  757.9 4.7 all-to-all-start.2
  763.4 10.4 scatter_custom_fusion
  773.8 60.4 %all-to-all-done.2 = bf16[8,2,96,2048]{3,2,1,0:T(8,128)(2,1)} async-done(((bf16[8,2,96,2048]{3,2,1,0:T(8,128)(2,1)}), bf16[8,2,96,2048]{3,2,1,0:T(8,128)(2,1)}, u32[]{:S(2)}, u32[]{:S(2)}) %all-to-all-start.2) | async-done | bytes 6291488 | tf_op jit(solution)/shard_map/all_to_all | solution.py:215
  834.2 4.8 all-to-all-start
  839.0 6.6 copy.95
  845.6 65.0 %all-to-all-done = bf16[8,2,96,2048]{3,2,1,0:T(8,128)(2,1)} async-done(((bf16[8,2,96,2048]{3,2,1,0:T(8,128)(2,1)}), bf16[8,2,96,2048]{3,2,1,0:T(8,128)(2,1)}, u32[]{:S(2)}, u32[]{:S(2)}) %all-to-all-start) | async-done | bytes 6291488 | tf_op jit(solution)/shard_map/all_to_all | solution.py:190
  910.6 6.7 copy.92
  917.3 10.4 fusion.103
  927.7 31.8 %all-gather.24.cloned.1.call-done = bf16[2,2048,768]{2,1,0:T(8,128)(2,1)} async-done(((bf16[2,512,768]{2,1,0:T(8,128)(2,1)}), bf16[2,2048,768]{2,1,0:T(8,128)(2,1)}) %all-gather.24.cloned.1.call-update) | async-done | bytes 6291472 | tf_op jit(solution)/shard_map/all_gather | solution.py:168
  959.5 10.4 fusion.104
  969.9 104.8 %all-gather.26.cloned.1.call-done = bf16[2,768,2048]{2,1,0:T(8,128)(2,1)} async-done(((bf16[2,192,2048]{2,1,0:T(8,128)(2,1)}), bf16[2,768,2048]{2,1,0:T(8,128)(2,1)}) %all-gather.26.cloned.1.call-update) | async-done | bytes 6291472 | tf_op jit(solution)/shard_map/all_gather | solution.py:169
  1074.6 13.9 multiply_convert_fusion.1
  1088.5 6.9 convert_bitcast_fusion
  1095.4 18.8 copy.93
  1114.2 5.2 all-to-all-start.1
  1119.4 10.7 fusion.105
  1130.2 10.2 fusion.58
  1140.4 18.8 copy.96
  1159.2 31.8 %all-to-all-done.1 = bf16[1,2,768,2048]{3,1,0,2:T(2,128)(2,1)} async-done(((bf16[1,2,768,2048]{3,1,0,2:T(2,128)(2,1)}), bf16[1,2,768,2048]{3,1,0,2:T(2,128)(2,1)}, u32[]{:S(2)}, u32[]{:S(2)}) %all-to-all-start.1) | async-done | bytes 6291488 | tf_op jit(solution)/shard_map/all_to_all | solution.py:203
  1191.0 4.7 all-to-all-start.3
  1195.9 8.3 copy.94
  1204.1 12.6 gather_fusion.3
  1216.7 5.5 fusion.61
  1224.9 42.5 %all-to-all-done.3 = bf16[1,2,768,2048]{3,1,0,2:T(2,128)(2,1)} async-done(((bf16[1,2,768,2048]{3,1,0,2:T(2,128)(2,1)}), bf16[1,2,768,2048]{3,1,0,2:T(2,128)(2,1)}, u32[]{:S(2)}, u32[]{:S(2)}) %all-to-all-start.3) | async-done | bytes 6291488 | tf_op jit(solution)/shard_map/all_to_all | solution.py:230
  1267.3 8.3 copy.97
  1275.6 12.6 gather_fusion.4
  1288.3 6.8 convert_reduce_fusion
  1298.3 12.7 fusion.72
  1314.0 60.3 %while.29 = (s32[]{:T(128)}, f32[4,8,128,128]{3,2,1,0:T(8,128)}, bf16[4,1024,128]{1,2,0:T(8,128)(2,1)}, bf16[4,1024,128]{1,2,0:T(8,128)(2,1)}, bf16[4,8,128,128]...) while((s32[]{:T(128)}, f32[4,8,128,128]{3,2,1,0:T(8,128)}, ...), condition=%wide.region_20.22_spmd.clone, body=%wide.region_18.21_spmd.clone.sunk | while | flops 1358691328 | bytes 52995752 | solution.py:268
  1370.2 4.1 fusion.181
  1379.2 30.1 %reduce-scatter.31.cloned.1.call-done = bf16[128,512]{1,0:T(8,128)(2,1)} async-done(((bf16[1024,512]{1,0:T(8,128)(2,1)}), bf16[128,512]{1,0:T(8,128)(2,1)}) %reduce-scatter.31.cloned.1.call-update) | async-done | bytes 131088
  1412.8 35.6 %reduce-scatter.33.cloned.1.call-done = bf16[128,512]{1,0:T(8,128)(2,1)} async-done(((bf16[1024,512]{1,0:T(8,128)(2,1)}), bf16[128,512]{1,0:T(8,128)(2,1)}) %reduce-scatter.33.cloned.1.call-update) | async-done | bytes 131088
  1451.6 9.4 convolution_convert_fusion
  1468.7 11.7 convolution_convert_fusion.1
  1482.5 9.7 convolution_convert_fusion.3
  1492.2 9.7 convolution_convert_fusion.5
  1502.0 9.9 convolution_convert_fusion.4
  1512.0 27.4 %reduce-scatter.19.cloned.1.call-done = bf16[512,512]{1,0:T(8,128)(2,1)} async-done(((bf16[2048,512]{1,0:T(8,128)(2,1)}), bf16[512,512]{1,0:T(8,128)(2,1)}) %reduce-scatter.19.cloned.1.call-update) | async-done | bytes 524304 | tf_op jit(solution)/shard_map/reduce_scatter | solution.py:327
  1539.4 281.9 %reduce-scatter.21.cloned.1.call-done = bf16[1024,2048]{1,0:T(8,128)(2,1)} async-done(((bf16[4096,2048]{1,0:T(8,128)(2,1)}), bf16[1024,2048]{1,0:T(8,128)(2,1)}) %reduce-scatter.21.cloned.1.call-update) | async-done | bytes 4194320 | tf_op jit(solution)/shard_map/reduce_scatter | solution.py:330
  1821.3 283.3 %reduce-scatter.15.cloned.1.call-done = bf16[512,4096]{1,0:T(8,128)(2,1)} async-done(((bf16[2048,4096]{1,0:T(8,128)(2,1)}), bf16[512,4096]{1,0:T(8,128)(2,1)}) %reduce-scatter.15.cloned.1.call-update) | async-done | bytes 4194320 | tf_op jit(solution)/shard_map/reduce_scatter | solution.py:321
  2105.8 11.5 fusion.106
  2117.4 9.8 reduce-scatter.23.cloned.1.call-done
  2127.2 23.7 psum.71
  2155.1 42.7 %all-reduce = (f32[2048]{0:T(1024)}, f32[128]{0:T(128)}, f32[128]{0:T(128)}, f32[2048]{0:T(1024)}) all-reduce(f32[2048]{0:T(1024)S(1)} %get-tuple-element.220, f32[128]{0:T(128)S(1)} %get-tuple-element.216, f32[128]{0:T(128)S(1)} %get-tuple-element.222, f32[2048]{0:T(1024)S(1)} %copy-done.57), channel_id=1, replica_groups=mesh['ctx'=8,'fsdp'=4] {'ctx','fsdp'}, use_global_device_ids=true, to_apply=%region_27.29 | all-reduce | flops 4352 | bytes 34816 | tf_op jit(solution)/shard_map/psum | solution.py:344
  2199.1 40.3 %reduce-scatter.29.cloned.1.call-done = bf16[2,192,2048]{2,1,0:T(8,128)(2,1)} async-done(((bf16[2,768,2048]{2,1,0:T(8,128)(2,1)}), bf16[2,192,2048]{2,1,0:T(8,128)(2,1)}) %reduce-scatter.29.cloned.1.call-update) | async-done | bytes 1572880 | tf_op jit(solution)/shard_map/reduce_scatter | solution.py:316
  2242.8 110.6 %reduce-scatter.25.cloned.1.call-done = bf16[2,512,768]{2,1,0:T(8,128)(2,1)} async-done(((bf16[2,2048,768]{2,1,0:T(8,128)(2,1)}), bf16[2,512,768]{2,1,0:T(8,128)(2,1)}) %reduce-scatter.25.cloned.1.call-update) | async-done | bytes 1572880 | tf_op jit(solution)/shard_map/reduce_scatter | solution.py:310
  2356.7 110.3 %reduce-scatter.27.cloned.1.call-done = bf16[2,512,768]{2,1,0:T(8,128)(2,1)} async-done(((bf16[2,2048,768]{2,1,0:T(8,128)(2,1)}), bf16[2,512,768]{2,1,0:T(8,128)(2,1)}) %reduce-scatter.27.cloned.1.call-update) | async-done | bytes 1572880 | tf_op jit(solution)/shard_map/reduce_scatter | solution.py:313
  2470.3 138.7 %all-reduce.4.cloned.1.call-done = (bf16[512,4096]{1,0:T(8,128)(2,1)}, bf16[512,512]{1,0:T(8,128)(2,1)}, bf16[512,512]{1,0:T(8,128)(2,1)}, bf16[1024,2048]{1,0:T(8,128)(2,1)}) async-done(((bf16[512,4096]{1,0:T(8,128)(2,1)}, bf16[512,512]{1,0:T(8,128)(2,1)}, bf16[512,512]{1,0:T(8,128)(2,1)}, bf16[1024,2048]{1,0:T(8,128)(2,1)}), (bf16[512,4096]{1,0:T(8,128)(2,1)}, bf16[512,512]{1,0:T(8,128)(2,1)}, ...) | async-done | bytes 9437200 | tf_op jit(solution)/shard_map/psum | solution.py:338
  2609.0 6.8 convert_element_type.218
  2615.9 4.5 convert_element_type.224
  (354 shorter events, 166.1 us)
Async XLA Ops:
  7.2 50.8 %all-gather.12.cloned.1.call-start = ((), (), s32[]{:S(2)}) async-start(), calls=%async_computation.15 | async-start | bytes 2621440 | tf_op jit(solution)/shard_map/all_gather | solution.py:109
  7.9 96.1 %all-gather.16.cloned.1.call-start = ((), (), s32[]{:S(2)}) async-start(), calls=%async_computation.17 | async-start | bytes 2621440 | tf_op jit(solution)/shard_map/all_gather | solution.py:110
  8.7 125.1 %all-gather.14.cloned.1.call-start = ((), (), s32[]{:S(2)}) async-start(), calls=%async_computation.16 | async-start | bytes 1179648 | tf_op jit(solution)/shard_map/all_gather | solution.py:127
  12.1 91.9 %copy-start.59 = (f32[128]{0:T(128)}, f32[128]{0:T(128)S(1)}, u32[]{:S(2)}) copy-start(f32[128]{0:T(128)S(1)} %add_rsqrt_fusion.3) | copy-start | bytes 1540
  12.9 463.0 %copy-start.29 = (f32[128,64]{0,1:T(8,128)}, f32[128,64]{0,1:T(8,128)S(1)}, u32[]{:S(2)}) copy-start(f32[128,64]{0,1:T(8,128)S(1)} %get-tuple-element.297) | copy-start | bytes 98308
  12.9 463.0 %copy-start.31 = (f32[128,64]{0,1:T(8,128)}, f32[128,64]{0,1:T(8,128)S(1)}, u32[]{:S(2)}) copy-start(f32[128,64]{0,1:T(8,128)S(1)} %get-tuple-element.298) | copy-start | bytes 98308
  12.9 51.5 %copy-start.61 = (f32[128]{0:T(128)S(1)}, f32[128]{0:T(128)}, u32[]{:S(2)}) copy-start(f32[128]{0:T(128)} %param.32) | copy-start | bytes 1540
  14.3 451.6 %copy-start.13 = (bf16[1,128,2048]{2,1,0:T(8,128)(2,1)}, bf16[1,128,2048]{2,1,0:T(8,128)(2,1)S(1)}, u32[]{:S(2)}) copy-start(bf16[1,128,2048]{2,1,0:T(8,128)(2,1)S(1)} %multiply_convert_fusion.7) | copy-start | bytes 1572868
  58.0 46.1 %copy-start.3 = (f32[1,128,2048]{2,1,0:T(8,128)S(1)}, f32[1,128,2048]{2,1,0:T(8,128)}, u32[]{:S(2)}) copy-start(f32[1,128,2048]{2,1,0:T(8,128)} %param.23) | copy-start | bytes 3145732
  58.0 46.1 %copy-start.46 = (f32[2048]{0:T(1024)S(1)}, f32[2048]{0:T(1024)}, u32[]{:S(2)}) copy-start(f32[2048]{0:T(1024)} %param.27) | copy-start | bytes 24580
  64.3 43.1 %copy-start.23 = (f32[128,4,128]{0,2,1:T(8,128)}, f32[128,4,128]{0,2,1:T(8,128)S(1)}, u32[]{:S(2)}) copy-start(f32[128,4,128]{0,2,1:T(8,128)S(1)} %get-tuple-element.304) | copy-start | bytes 786436
  64.4 43.1 %copy-start.55 = (f32[128,4]{0,1:T(4,128)}, f32[128,4]{0,1:T(4,128)S(1)}, u32[]{:S(2)}) copy-start(f32[128,4]{0,1:T(4,128)S(1)} %add_rsqrt_fusion.1) | copy-start | bytes 6148
  65.2 89.4 %all-gather.18.cloned.1.call-start = ((), (), s32[]{:S(2)}) async-start(), calls=%async_computation.18 | async-start | bytes 1179648 | tf_op jit(solution)/shard_map/all_gather | solution.py:128
  106.9 336.0 %all-gather.10.cloned.1.call-start = ((), (), s32[]{:S(2)}) async-start(), calls=%async_computation.14 | async-start | bytes 20971520 | tf_op jit(solution)/shard_map/all_gather | solution.py:108
  107.5 621.7 %all-gather.20.cloned.1.call-start = ((), (), s32[]{:S(2)}) async-start(), calls=%async_computation.19 | async-start | bytes 20971520 | tf_op jit(solution)/shard_map/all_gather | solution.py:111
  108.1 809.2 %all-gather.22.cloned.1.call-start = ((), (), s32[]{:S(2)}) async-start(), calls=%async_computation.20 | async-start | bytes 7864320 | tf_op jit(solution)/shard_map/all_gather | solution.py:167
  108.8 850.7 %all-gather.24.cloned.1.call-start = ((), (), s32[]{:S(2)}) async-start(), calls=%async_computation.21 | async-start | bytes 7864320 | tf_op jit(solution)/shard_map/all_gather | solution.py:168
  109.9 23.8 copy-start.26
  128.3 610.7 %copy-start.33 = (bf16[2048,16]{0,1:T(8,128)(2,1)}, bf16[2048,16]{0,1:T(8,128)(2,1)S(1)}, u32[]{:S(2)}) copy-start(bf16[2048,16]{0,1:T(8,128)(2,1)S(1)} %all_gather.42) | copy-start | bytes 196612
  133.7 332.2 %copy-start.50 = (s32[1024]{0:T(1024)}, s32[1024]{0:T(1024)S(1)}, u32[]{:S(2)}) copy-start(s32[1024]{0:T(1024)S(1)} %fusion.88) | copy-start | bytes 12292
  465.9 9.6 copy-start.63
  508.0 229.7 %copy-start.7 = (bf16[4,1024,128]{2,1,0:T(8,128)(2,1)}, bf16[4,1024,128]{2,1,0:T(8,128)(2,1)S(1)}, u32[]{:S(2)}) copy-start(bf16[4,1024,128]{2,1,0:T(8,128)(2,1)S(1)} %get-tuple-element.573) | copy-start | bytes 3145732
  508.0 229.7 %copy-start.15 = (bf16[4,8,128,128]{3,2,1,0:T(8,128)(2,1)}, bf16[4,8,128,128]{3,2,1,0:T(8,128)(2,1)S(1)}, u32[]{:S(2)}) copy-start(bf16[4,8,128,128]{3,2,1,0:T(8,128)(2,1)S(1)} %get-tuple-element.574) | copy-start | bytes 3145732
  508.0 229.8 %copy-start.35 = (s32[1024]{0:T(1024)}, s32[1024]{0:T(1024)S(1)}, u32[]{:S(2)}) copy-start(s32[1024]{0:T(1024)S(1)} %get-tuple-element.615) | copy-start | bytes 12292
  508.0 229.8 %copy-start.40 = (s32[1024]{0:T(1024)}, s32[1024]{0:T(1024)S(1)}, u32[]{:S(2)}) copy-start(s32[1024]{0:T(1024)S(1)} %get-tuple-element.631) | copy-start | bytes 12292
  508.0 229.8 %copy-start.52 = (s32[128]{0:T(128)}, s32[128]{0:T(128)S(1)}, u32[]{:S(2)}) copy-start(s32[128]{0:T(128)S(1)} %get-tuple-element.635) | copy-start | bytes 1540
  729.2 9.6 copy-start.48
  739.0 24.4 copy-start.19
  739.2 7.3 copy-start.27
  739.2 8.0 copy-start.25
  757.9 76.3 %all-to-all-start.2 = ((bf16[8,2,96,2048]{3,2,1,0:T(8,128)(2,1)}), bf16[8,2,96,2048]{3,2,1,0:T(8,128)(2,1)}, u32[]{:S(2)}, u32[]{:S(2)}) async-start(bf16[8,2,96,2048]{3,2,1,0:T(8,128)(2,1)} %bitcast.321), calls=%async_computation.2 | async-start | bytes 12582912 | tf_op jit(solution)/shard_map/all_to_all | solution.py:215
  762.7 312.0 %all-gather.26.cloned.1.call-start = ((), (), s32[]{:S(2)}) async-start(), calls=%async_computation.22 | async-start | bytes 7864320 | tf_op jit(solution)/shard_map/all_gather | solution.py:169
  834.2 76.4 %all-to-all-start = ((bf16[8,2,96,2048]{3,2,1,0:T(8,128)(2,1)}), bf16[8,2,96,2048]{3,2,1,0:T(8,128)(2,1)}, u32[]{:S(2)}, u32[]{:S(2)}) async-start(bf16[8,2,96,2048]{3,2,1,0:T(8,128)(2,1)} %bitcast.322), calls=%async_computation | async-start | bytes 12582912 | tf_op jit(solution)/shard_map/all_to_all | solution.py:190
  1074.6 13.9 copy-start.67
  1114.2 76.8 %all-to-all-start.1 = ((bf16[1,2,768,2048]{3,1,0,2:T(2,128)(2,1)}), bf16[1,2,768,2048]{3,1,0,2:T(2,128)(2,1)}, u32[]{:S(2)}, u32[]{:S(2)}) async-start(bf16[1,2,768,2048]{3,1,0,2:T(2,128)(2,1)} %copy.93), calls=%async_computation.1 | async-start | bytes 12582912 | tf_op jit(solution)/shard_map/all_to_all | solution.py:203
  1119.4 10.7 copy-start.69
  1159.2 36.7 %copy-start.51 = (s32[1024]{0:T(1024)S(1)}, s32[1024]{0:T(1024)}, u32[]{:S(2)}) copy-start(s32[1024]{0:T(1024)} %copy-done.50) | copy-start | bytes 12292
  1191.0 76.3 %all-to-all-start.3 = ((bf16[1,2,768,2048]{3,1,0,2:T(2,128)(2,1)}), bf16[1,2,768,2048]{3,1,0,2:T(2,128)(2,1)}, u32[]{:S(2)}, u32[]{:S(2)}) async-start(bf16[1,2,768,2048]{3,1,0,2:T(2,128)(2,1)} %copy.96), calls=%async_computation.3 | async-start | bytes 12582912 | tf_op jit(solution)/shard_map/all_to_all | solution.py:230
  1195.7 213.5 %reduce-scatter.31.cloned.1.call-start = ((), (), s32[]{:S(2)}) async-start(), calls=%async_computation.31 | async-start | bytes 1179648
  1288.2 7.2 copy-start.12
  1288.2 7.2 copy-start.34
  1288.3 8.3 copy-start.28
  1298.3 153.3 %copy-start.9 = (f32[128,2048]{1,0:T(8,128)}, f32[128,2048]{1,0:T(8,128)S(1)}, u32[]{:S(2)}) copy-start(f32[128,2048]{1,0:T(8,128)S(1)} %get-tuple-element.291) | copy-start | bytes 3145732
  1374.3 36.0 %copy-start.30 = (f32[128,64]{0,1:T(8,128)S(1)}, f32[128,64]{0,1:T(8,128)}, u32[]{:S(2)}) copy-start(f32[128,64]{0,1:T(8,128)} %copy-done.29) | copy-start | bytes 98308
  1374.3 36.0 %copy-start.32 = (f32[128,64]{0,1:T(8,128)S(1)}, f32[128,64]{0,1:T(8,128)}, u32[]{:S(2)}) copy-start(f32[128,64]{0,1:T(8,128)} %copy-done.31) | copy-start | bytes 98308
  1374.3 36.0 %copy-start.24 = (f32[128,4,128]{0,2,1:T(8,128)S(1)}, f32[128,4,128]{0,2,1:T(8,128)}, u32[]{:S(2)}) copy-start(f32[128,4,128]{0,2,1:T(8,128)} %copy-done.23) | copy-start | bytes 786436
  1374.3 36.0 %copy-start.56 = (f32[128,4]{0,1:T(4,128)S(1)}, f32[128,4]{0,1:T(4,128)}, u32[]{:S(2)}) copy-start(f32[128,4]{0,1:T(4,128)} %copy-done.55) | copy-start | bytes 6148
  1374.3 36.0 %copy-start.62 = (f32[128]{0:T(128)S(1)}, f32[128]{0:T(128)}, u32[]{:S(2)}) copy-start(f32[128]{0:T(128)} %param.32) | copy-start | bytes 1540
  1374.4 36.3 %copy-start.14 = (bf16[1,128,2048]{2,1,0:T(8,128)(2,1)S(1)}, bf16[1,128,2048]{2,1,0:T(8,128)(2,1)}, u32[]{:S(2)}) copy-start(bf16[1,128,2048]{2,1,0:T(8,128)(2,1)} %copy-done.13) | copy-start | bytes 1572868
  1376.7 71.7 %reduce-scatter.33.cloned.1.call-start = ((), (), s32[]{:S(2)}) async-start(), calls=%async_computation.32 | async-start | bytes 1179648
  1379.1 69.3 %copy-start.4 = (f32[1,128,2048]{2,1,0:T(8,128)S(1)}, f32[1,128,2048]{2,1,0:T(8,128)}, u32[]{:S(2)}) copy-start(f32[1,128,2048]{2,1,0:T(8,128)} %param.23) | copy-start | bytes 3145732
  1379.1 69.3 %copy-start.47 = (f32[2048]{0:T(1024)S(1)}, f32[2048]{0:T(1024)}, u32[]{:S(2)}) copy-start(f32[2048]{0:T(1024)} %param.27) | copy-start | bytes 24580
  1379.1 69.3 %copy-start.60 = (f32[128]{0:T(128)S(1)}, f32[128]{0:T(128)}, u32[]{:S(2)}) copy-start(f32[128]{0:T(128)} %copy-done.59) | copy-start | bytes 1540
  1379.1 132.9 %reduce-scatter.17.cloned.1.call-start = ((), (), s32[]{:S(2)}) async-start(), calls=%async_computation.24 | async-start | bytes 2621440 | tf_op jit(solution)/shard_map/reduce_scatter | solution.py:324
  1412.8 126.6 %reduce-scatter.19.cloned.1.call-start = ((), (), s32[]{:S(2)}) async-start(), calls=%async_computation.25 | async-start | bytes 2621440 | tf_op jit(solution)/shard_map/reduce_scatter | solution.py:327
  1451.5 369.8 %reduce-scatter.21.cloned.1.call-start = ((), (), s32[]{:S(2)}) async-start(), calls=%async_computation.26 | async-start | bytes 20971520 | tf_op jit(solution)/shard_map/reduce_scatter | solution.py:330
  1461.0 643.6 %reduce-scatter.15.cloned.1.call-start = ((), (), s32[]{:S(2)}) async-start(), calls=%async_computation.23 | async-start | bytes 20971520 | tf_op jit(solution)/shard_map/reduce_scatter | solution.py:321
  1480.5 646.7 %reduce-scatter.23.cloned.1.call-start = ((), (), s32[]{:S(2)}) async-start(), calls=%async_computation.27 | async-start | bytes 81920 | tf_op jit(solution)/shard_map/reduce_scatter | solution.py:333
  1482.4 757.0 %reduce-scatter.29.cloned.1.call-start = ((), (), s32[]{:S(2)}) async-start(), calls=%async_computation.30 | async-start | bytes 7864320 | tf_op jit(solution)/shard_map/reduce_scatter | solution.py:316
  1492.2 861.2 %reduce-scatter.25.cloned.1.call-start = ((), (), s32[]{:S(2)}) async-start(), calls=%async_computation.28 | async-start | bytes 7864320 | tf_op jit(solution)/shard_map/reduce_scatter | solution.py:310
  1502.0 965.1 %reduce-scatter.27.cloned.1.call-start = ((), (), s32[]{:S(2)}) async-start(), calls=%async_computation.29 | async-start | bytes 7864320 | tf_op jit(solution)/shard_map/reduce_scatter | solution.py:313
  1511.9 1097.1 %all-reduce.4.cloned.1.call-start = ((), (), s32[]{:S(2)}) async-start(), calls=%async_computation.33 | async-start | bytes 18874368 | tf_op jit(solution)/shard_map/psum | solution.py:338
  2117.4 36.8 %copy-start.39 = (bf16[128,512]{1,0:T(8,128)(2,1)S(1)}, bf16[128,512]{1,0:T(8,128)(2,1)}, u32[]{:S(2)}) copy-start(bf16[128,512]{1,0:T(8,128)(2,1)} %reduce-scatter.33.cloned.1.call-done) | copy-start | bytes 393220
  2151.6 46.2 %copy-start.10 = (f32[128,2048]{1,0:T(8,128)S(1)}, f32[128,2048]{1,0:T(8,128)}, u32[]{:S(2)}) copy-start(f32[128,2048]{1,0:T(8,128)} %copy-done.9) | copy-start | bytes 3145732
  (33 other events, 121.5 us)
Sparse Core Ops, SparseCore 0:
  9.6 48.3 all-gather.11
  59.6 44.4 all-gather.15
  106.5 22.2 all-gather.13
  131.1 23.4 all-gather.17
  156.0 286.7 all-gather.9
  444.2 284.9 all-gather.19
  730.8 113.5 all-gather.21
  845.9 113.5 all-gather.23
  961.1 113.5 all-gather.25
  1376.9 32.3 reduce-scatter.30
  1412.4 35.9 reduce-scatter.32
  1450.6 43.6 reduce-scatter.16
  1496.5 42.8 reduce-scatter.18
  1541.6 279.6 reduce-scatter.20
  1823.5 281.0 reduce-scatter.14
  2107.3 19.9 reduce-scatter.22
  2129.4 109.9 reduce-scatter.28
  2242.1 111.2 reduce-scatter.24
  2355.7 111.2 reduce-scatter.26
  2470.8 138.1 all-reduce.3
where the time goes:
time: 2640 us; the launch traced here: 2630 us
  waiting for transfers between devices  2020 us (77%)
  matrix products  236 us (9%)
  local copies, waits for them, and re-layouts  178 us (7%)
  other arithmetic  81.3 us (3%)
  blocking collectives  80 us (3%)
    all_gather x1, waiting for transfers between devices, per_device(): lax.all_gather(query_proj, 'fsdp', axis=0, tiled=True)  286 us
    reduce_scatter x1, waiting for transfers between devices, per_device(): lax.psum_scatter(query_grad_full.astype(jnp.bfloat16), 'fsdp', scatter_di...  283 us
    reduce_scatter x1, waiting for transfers between devices, per_device(): lax.psum_scatter(out_grad_full.astype(jnp.bfloat16), 'fsdp', scatter_dime...  282 us
    all_gather x1, waiting for transfers between devices, per_device(): lax.all_gather(out_proj, 'fsdp', axis=0, tiled=True)  221 us
    dot_general x47, matrix products, contract(): return jnp.einsum(form, left, right, preferred_element_type=jnp.float32)  206 us
    psum x1, waiting for transfers between devices, per_device(): lax.psum(shard_grads[0].astype(jnp.bfloat16), 'ctx').astype(jnp.float32)  139 us
    reduce_scatter x1, waiting for transfers between devices, per_device(): lax.psum_scatter(gate_grad_full.astype(jnp.bfloat16), 'fsdp', scatter_dim...  111 us
    reduce_scatter x1, waiting for transfers between devices, per_device(): lax.psum_scatter(up_grad_full.astype(jnp.bfloat16), 'fsdp', scatter_dimen...  110 us
  transfers between devices with their start and end apart: 24, of which 21 were waited for; matrix products, arithmetic and copies ran while one was open for 13% of the time, Pallas kernels for 0%

commit v1 on v0

--- a/solution.py
+++ b/solution.py
@@ -335,7 +335,9 @@
         ).astype(jnp.float32),
     )
     query_grad, key_grad, value_grad, out_grad, router_grad = (
-        lax.psum(shard_grads[0].astype(jnp.bfloat16), "ctx").astype(jnp.float32),
+        jnp.sum(lax.all_gather(shard_grads[0].astype(jnp.bfloat16), "ctx"), axis=0).astype(
+            jnp.float32
+        ),
         lax.psum(shard_grads[1].astype(jnp.bfloat16), "ctx").astype(jnp.float32),
         lax.psum(shard_grads[2].astype(jnp.bfloat16), "ctx").astype(jnp.float32),
         lax.psum(shard_grads[3].astype(jnp.bfloat16), "ctx").astype(jnp.float32),

time: 2640 us -> 2760 us (1.045)
  waiting for transfers between devices: 2020 us -> 2130 us
    all_gather x0 -> x1, waiting for transfers between devices: none -> 154 us  [per_device(): lax.all_gather(shard_grads[0].astype(jnp.bfloat16), 'ctx')]
    psum x1, waiting for transfers between devices: 139 us -> 93 us  [per_device(): lax.psum(shard_grads[1].astype(jnp.bfloat16), 'ctx').astype(jnp.float32)]
    unnamed x22 -> x23, waiting for transfers between devices: 70.4 us -> 70.4 us
  transfers between devices with their start and end apart: 24 -> 25, of which waited for: 21 -> 22; matrix products, arithmetic and copies ran while one was open for 13% -> 12% of each run, Pallas kernels for 0% -> 0%
where the time goes in v1:
time: 2760 us; the launch traced here: 2750 us
  waiting for transfers between devices  2130 us (77%)
  matrix products  236 us (9%)
  local copies, waits for them, and re-layouts  177 us (6%)
  other arithmetic  98 us (4%)
  blocking collectives  80 us (3%)
    all_gather x1, waiting for transfers between devices, per_device(): lax.all_gather(query_proj, 'fsdp', axis=0, tiled=True)  286 us
    reduce_scatter x1, waiting for transfers between devices, per_device(): lax.psum_scatter(query_grad_full.astype(jnp.bfloat16), 'fsdp', scatter_di...  283 us
    reduce_scatter x1, waiting for transfers between devices, per_device(): lax.psum_scatter(out_grad_full.astype(jnp.bfloat16), 'fsdp', scatter_dime...  282 us
    all_gather x1, waiting for transfers between devices, per_device(): lax.all_gather(out_proj, 'fsdp', axis=0, tiled=True)  221 us
    dot_general x47, matrix products, contract(): return jnp.einsum(form, left, right, preferred_element_type=jnp.float32)  206 us
    all_gather x1, waiting for transfers between devices, per_device(): lax.all_gather(shard_grads[0].astype(jnp.bfloat16), 'ctx')  154 us
    reduce_scatter x1, waiting for transfers between devices, per_device(): lax.psum_scatter(gate_grad_full.astype(jnp.bfloat16), 'fsdp', scatter_dim...  111 us
    reduce_scatter x1, waiting for transfers between devices, per_device(): lax.psum_scatter(up_grad_full.astype(jnp.bfloat16), 'fsdp', scatter_dimen...  110 us
  transfers between devices with their start and end apart: 25, of which 22 were waited for; matrix products, arithmetic and copies ran while one was open for 12% of the time, Pallas kernels for 0%

profile of v1, /device:TPU:0, one launch (start us, length us, event | category | flops | bytes accessed | tf_op | source)
XLA Modules:
  0.0 2754.2 jit_solution(14238966790512579599)
XLA Ops:
  14.3 43.6 %all-gather.14.cloned.1.call-done = bf16[2048,512]{1,0:T(8,128)(2,1)} async-done(((bf16[512,512]{1,0:T(8,128)(2,1)}), bf16[2048,512]{1,0:T(8,128)(2,1)}) %all-gather.14.cloned.1.call-update) | async-done | bytes 2097168 | tf_op jit(solution)/shard_map/all_gather | solution.py:109
  65.3 38.8 %all-gather.18.cloned.1.call-done = bf16[2048,512]{1,0:T(8,128)(2,1)} async-done(((bf16[512,512]{1,0:T(8,128)(2,1)}), bf16[2048,512]{1,0:T(8,128)(2,1)}) %all-gather.18.cloned.1.call-update) | async-done | bytes 2097168 | tf_op jit(solution)/shard_map/all_gather | solution.py:110
  110.2 4.5 gather_fusion
  114.7 13.7 all_gather.48
  135.5 19.1 all-gather.20.cloned.1.call-done
  156.9 285.8 %all-gather.12.cloned.1.call-done = bf16[2048,4096]{1,0:T(8,128)(2,1)} async-done(((bf16[512,4096]{1,0:T(8,128)(2,1)}), bf16[2048,4096]{1,0:T(8,128)(2,1)}) %all-gather.12.cloned.1.call-update) | async-done | bytes 16777232 | tf_op jit(solution)/shard_map/all_gather | solution.py:108
  442.7 23.1 copy.78
  465.8 8.3 multiply_reduce_fusion.3
  480.9 27.2 while.28
  508.1 221.0 %all-gather.22.cloned.1.call-done = bf16[4096,2048]{1,0:T(8,128)(2,1)} async-done(((bf16[1024,2048]{1,0:T(8,128)(2,1)}), bf16[4096,2048]{1,0:T(8,128)(2,1)}) %all-gather.22.cloned.1.call-update) | async-done | bytes 16777232 | tf_op jit(solution)/shard_map/all_gather | solution.py:111
  729.2 8.6 multiply_reduce_fusion.8
  739.2 7.2 gather_fusion.2
  747.2 10.7 scatter_custom_fusion.1
  757.8 4.7 all-to-all-start.2
  763.3 10.4 scatter_custom_fusion
  773.8 60.4 %all-to-all-done.2 = bf16[8,2,96,2048]{3,2,1,0:T(8,128)(2,1)} async-done(((bf16[8,2,96,2048]{3,2,1,0:T(8,128)(2,1)}), bf16[8,2,96,2048]{3,2,1,0:T(8,128)(2,1)}, u32[]{:S(2)}, u32[]{:S(2)}) %all-to-all-start.2) | async-done | bytes 6291488 | tf_op jit(solution)/shard_map/all_to_all | solution.py:215
  834.2 4.8 all-to-all-start
  838.9 6.6 copy.95
  845.6 65.0 %all-to-all-done = bf16[8,2,96,2048]{3,2,1,0:T(8,128)(2,1)} async-done(((bf16[8,2,96,2048]{3,2,1,0:T(8,128)(2,1)}), bf16[8,2,96,2048]{3,2,1,0:T(8,128)(2,1)}, u32[]{:S(2)}, u32[]{:S(2)}) %all-to-all-start) | async-done | bytes 6291488 | tf_op jit(solution)/shard_map/all_to_all | solution.py:190
  910.5 6.7 copy.92
  917.2 10.5 fusion.103
  927.7 31.7 %all-gather.26.cloned.1.call-done = bf16[2,2048,768]{2,1,0:T(8,128)(2,1)} async-done(((bf16[2,512,768]{2,1,0:T(8,128)(2,1)}), bf16[2,2048,768]{2,1,0:T(8,128)(2,1)}) %all-gather.26.cloned.1.call-update) | async-done | bytes 6291472 | tf_op jit(solution)/shard_map/all_gather | solution.py:168
  959.4 10.3 fusion.104
  969.8 104.8 %all-gather.28.cloned.1.call-done = bf16[2,768,2048]{2,1,0:T(8,128)(2,1)} async-done(((bf16[2,192,2048]{2,1,0:T(8,128)(2,1)}), bf16[2,768,2048]{2,1,0:T(8,128)(2,1)}) %all-gather.28.cloned.1.call-update) | async-done | bytes 6291472 | tf_op jit(solution)/shard_map/all_gather | solution.py:169
  1074.6 13.9 multiply_convert_fusion.1
  1088.4 6.9 convert_bitcast_fusion
  1095.3 18.8 copy.93
  1114.2 5.2 all-to-all-start.1
  1119.4 10.7 fusion.105
  1130.1 10.2 fusion.58
  1140.3 18.8 copy.96
  1159.1 31.8 %all-to-all-done.1 = bf16[1,2,768,2048]{3,1,0,2:T(2,128)(2,1)} async-done(((bf16[1,2,768,2048]{3,1,0,2:T(2,128)(2,1)}), bf16[1,2,768,2048]{3,1,0,2:T(2,128)(2,1)}, u32[]{:S(2)}, u32[]{:S(2)}) %all-to-all-start.1) | async-done | bytes 6291488 | tf_op jit(solution)/shard_map/all_to_all | solution.py:203
  1190.9 4.8 all-to-all-start.3
  1195.8 8.4 copy.94
  1204.2 12.6 gather_fusion.3
  1216.7 5.5 fusion.61
  1224.8 42.4 %all-to-all-done.3 = bf16[1,2,768,2048]{3,1,0,2:T(2,128)(2,1)} async-done(((bf16[1,2,768,2048]{3,1,0,2:T(2,128)(2,1)}), bf16[1,2,768,2048]{3,1,0,2:T(2,128)(2,1)}, u32[]{:S(2)}, u32[]{:S(2)}) %all-to-all-start.3) | async-done | bytes 6291488 | tf_op jit(solution)/shard_map/all_to_all | solution.py:230
  1267.3 8.4 copy.97
  1275.6 12.6 gather_fusion.4
  1288.3 6.8 convert_reduce_fusion
  1298.3 12.7 fusion.72
  1314.0 60.4 %while.29 = (s32[]{:T(128)}, f32[4,8,128,128]{3,2,1,0:T(8,128)}, bf16[4,1024,128]{1,2,0:T(8,128)(2,1)}, bf16[4,1024,128]{1,2,0:T(8,128)(2,1)}, bf16[4,8,128,128]...) while((s32[]{:T(128)}, f32[4,8,128,128]{3,2,1,0:T(8,128)}, ...), condition=%wide.region_20.22_spmd.clone, body=%wide.region_18.21_spmd.clone.sunk | while | flops 1358691328 | bytes 52995752 | solution.py:268
  1379.3 30.1 %reduce-scatter.31.cloned.1.call-done = bf16[128,512]{1,0:T(8,128)(2,1)} async-done(((bf16[1024,512]{1,0:T(8,128)(2,1)}), bf16[128,512]{1,0:T(8,128)(2,1)}) %reduce-scatter.31.cloned.1.call-update) | async-done | bytes 131088
  1413.0 35.6 %reduce-scatter.33.cloned.1.call-done = bf16[128,512]{1,0:T(8,128)(2,1)} async-done(((bf16[1024,512]{1,0:T(8,128)(2,1)}), bf16[128,512]{1,0:T(8,128)(2,1)}) %reduce-scatter.33.cloned.1.call-update) | async-done | bytes 131088
  1451.7 9.3 convolution_convert_fusion
  1468.8 11.7 convolution_convert_fusion.1
  1482.5 9.7 convolution_convert_fusion.3
  1492.2 9.7 convolution_convert_fusion.5
  1502.0 9.9 convolution_convert_fusion.4
  1512.0 27.5 reduce-scatter.19.cloned.1.call-done
  1539.5 281.9 %reduce-scatter.21.cloned.1.call-done = bf16[1024,2048]{1,0:T(8,128)(2,1)} async-done(((bf16[4096,2048]{1,0:T(8,128)(2,1)}), bf16[1024,2048]{1,0:T(8,128)(2,1)}) %reduce-scatter.21.cloned.1.call-update) | async-done | bytes 4194320 | tf_op jit(solution)/shard_map/reduce_scatter | solution.py:330
  1821.5 283.2 %reduce-scatter.15.cloned.1.call-done = bf16[512,4096]{1,0:T(8,128)(2,1)} async-done(((bf16[2048,4096]{1,0:T(8,128)(2,1)}), bf16[512,4096]{1,0:T(8,128)(2,1)}) %reduce-scatter.15.cloned.1.call-update) | async-done | bytes 4194320 | tf_op jit(solution)/shard_map/reduce_scatter | solution.py:321
  2104.8 11.5 fusion.106
  2116.3 11.0 reduce-scatter.23.cloned.1.call-done
  2127.3 23.7 psum.63
  2155.3 42.6 %all-reduce = (f32[2048]{0:T(1024)}, f32[128]{0:T(128)}, f32[128]{0:T(128)}, f32[2048]{0:T(1024)}) all-reduce(f32[2048]{0:T(1024)S(1)} %get-tuple-element.220, f32[128]{0:T(128)S(1)} %get-tuple-element.216, f32[128]{0:T(128)S(1)} %get-tuple-element.222, f32[2048]{0:T(1024)S(1)} %copy-done.56), channel_id=1, replica_groups=mesh['ctx'=8,'fsdp'=4] {'ctx','fsdp'}, use_global_device_ids=true, to_apply=%region_27.29 | all-reduce | flops 4352 | bytes 34816 | tf_op jit(solution)/shard_map/psum | solution.py:346
  2199.2 40.3 %reduce-scatter.29.cloned.1.call-done = bf16[2,192,2048]{2,1,0:T(8,128)(2,1)} async-done(((bf16[2,768,2048]{2,1,0:T(8,128)(2,1)}), bf16[2,192,2048]{2,1,0:T(8,128)(2,1)}) %reduce-scatter.29.cloned.1.call-update) | async-done | bytes 1572880 | tf_op jit(solution)/shard_map/reduce_scatter | solution.py:316
  2242.9 110.6 %reduce-scatter.25.cloned.1.call-done = bf16[2,512,768]{2,1,0:T(8,128)(2,1)} async-done(((bf16[2,2048,768]{2,1,0:T(8,128)(2,1)}), bf16[2,512,768]{2,1,0:T(8,128)(2,1)}) %reduce-scatter.25.cloned.1.call-update) | async-done | bytes 1572880 | tf_op jit(solution)/shard_map/reduce_scatter | solution.py:310
  2356.8 110.3 %reduce-scatter.27.cloned.1.call-done = bf16[2,512,768]{2,1,0:T(8,128)(2,1)} async-done(((bf16[2,2048,768]{2,1,0:T(8,128)(2,1)}), bf16[2,512,768]{2,1,0:T(8,128)(2,1)}) %reduce-scatter.27.cloned.1.call-update) | async-done | bytes 1572880 | tf_op jit(solution)/shard_map/reduce_scatter | solution.py:313
  2470.4 93.0 %all-reduce.4.cloned.1.call-done = (bf16[512,512]{1,0:T(8,128)(2,1)}, bf16[512,512]{1,0:T(8,128)(2,1)}, bf16[1024,2048]{1,0:T(8,128)(2,1)}) async-done(((bf16[512,512]{1,0:T(8,128)(2,1)}, bf16[512,512]{1,0:T(8,128)(2,1)}, bf16[1024,2048]{1,0:T(8,128)(2,1)}), (bf16[512,512]{1,0:T(8,128)(2,1)}, bf16[512,512]{1,0:T(8,128)(2,1)}, bf16[1024,2048]{1,0:T(8,128)(2,1)})) %all-reduce.4.cloned.1.call-update) | async-done | bytes 5242896 | tf_op jit(solution)/shard_map/psum | solution.py:341
  2563.5 6.7 convert_element_type.226
  2572.4 153.7 %all-gather.30.cloned.1.call-done = bf16[4096,4096]{1,0:T(8,128)(2,1)} async-done(((bf16[512,4096]{1,0:T(8,128)(2,1)}), bf16[4096,4096]{1,0:T(8,128)(2,1)}) %all-gather.30.cloned.1.call-update) | async-done | bytes 33554448 | tf_op jit(solution)/shard_map/all_gather | solution.py:338
  2726.2 14.2 reduce_sum.190
  2740.4 6.7 convert_element_type.220
  (356 shorter events, 173.9 us)
Async XLA Ops:
  7.2 50.8 %all-gather.14.cloned.1.call-start = ((), (), s32[]{:S(2)}) async-start(), calls=%async_computation.15 | async-start | bytes 2621440 | tf_op jit(solution)/shard_map/all_gather | solution.py:109
  7.9 96.1 %all-gather.18.cloned.1.call-start = ((), (), s32[]{:S(2)}) async-start(), calls=%async_computation.17 | async-start | bytes 2621440 | tf_op jit(solution)/shard_map/all_gather | solution.py:110
  8.7 125.1 %all-gather.16.cloned.1.call-start = ((), (), s32[]{:S(2)}) async-start(), calls=%async_computation.16 | async-start | bytes 1179648 | tf_op jit(solution)/shard_map/all_gather | solution.py:127
  12.1 91.9 %copy-start.58 = (f32[128]{0:T(128)}, f32[128]{0:T(128)S(1)}, u32[]{:S(2)}) copy-start(f32[128]{0:T(128)S(1)} %add_rsqrt_fusion.3) | copy-start | bytes 1540
  12.9 462.9 %copy-start.28 = (f32[128,64]{0,1:T(8,128)}, f32[128,64]{0,1:T(8,128)S(1)}, u32[]{:S(2)}) copy-start(f32[128,64]{0,1:T(8,128)S(1)} %get-tuple-element.296) | copy-start | bytes 98308
  12.9 462.9 %copy-start.30 = (f32[128,64]{0,1:T(8,128)}, f32[128,64]{0,1:T(8,128)S(1)}, u32[]{:S(2)}) copy-start(f32[128,64]{0,1:T(8,128)S(1)} %get-tuple-element.297) | copy-start | bytes 98308
  12.9 51.4 %copy-start.60 = (f32[128]{0:T(128)S(1)}, f32[128]{0:T(128)}, u32[]{:S(2)}) copy-start(f32[128]{0:T(128)} %param.32) | copy-start | bytes 1540
  14.3 451.5 %copy-start.13 = (bf16[1,128,2048]{2,1,0:T(8,128)(2,1)}, bf16[1,128,2048]{2,1,0:T(8,128)(2,1)S(1)}, u32[]{:S(2)}) copy-start(bf16[1,128,2048]{2,1,0:T(8,128)(2,1)S(1)} %multiply_convert_fusion.7) | copy-start | bytes 1572868
  58.0 46.1 %copy-start.3 = (f32[1,128,2048]{2,1,0:T(8,128)S(1)}, f32[1,128,2048]{2,1,0:T(8,128)}, u32[]{:S(2)}) copy-start(f32[1,128,2048]{2,1,0:T(8,128)} %param.23) | copy-start | bytes 3145732
  58.0 46.1 %copy-start.45 = (f32[2048]{0:T(1024)S(1)}, f32[2048]{0:T(1024)}, u32[]{:S(2)}) copy-start(f32[2048]{0:T(1024)} %param.27) | copy-start | bytes 24580
  64.3 43.1 %copy-start.22 = (f32[128,4,128]{0,2,1:T(8,128)}, f32[128,4,128]{0,2,1:T(8,128)S(1)}, u32[]{:S(2)}) copy-start(f32[128,4,128]{0,2,1:T(8,128)S(1)} %get-tuple-element.303) | copy-start | bytes 786436
  64.4 43.1 %copy-start.54 = (f32[128,4]{0,1:T(4,128)}, f32[128,4]{0,1:T(4,128)S(1)}, u32[]{:S(2)}) copy-start(f32[128,4]{0,1:T(4,128)S(1)} %add_rsqrt_fusion.1) | copy-start | bytes 6148
  65.2 89.4 %all-gather.20.cloned.1.call-start = ((), (), s32[]{:S(2)}) async-start(), calls=%async_computation.18 | async-start | bytes 1179648 | tf_op jit(solution)/shard_map/all_gather | solution.py:128
  106.9 335.9 %all-gather.12.cloned.1.call-start = ((), (), s32[]{:S(2)}) async-start(), calls=%async_computation.14 | async-start | bytes 20971520 | tf_op jit(solution)/shard_map/all_gather | solution.py:108
  107.5 621.7 %all-gather.22.cloned.1.call-start = ((), (), s32[]{:S(2)}) async-start(), calls=%async_computation.19 | async-start | bytes 20971520 | tf_op jit(solution)/shard_map/all_gather | solution.py:111
  108.1 809.1 %all-gather.24.cloned.1.call-start = ((), (), s32[]{:S(2)}) async-start(), calls=%async_computation.20 | async-start | bytes 7864320 | tf_op jit(solution)/shard_map/all_gather | solution.py:167
  108.8 850.6 %all-gather.26.cloned.1.call-start = ((), (), s32[]{:S(2)}) async-start(), calls=%async_computation.21 | async-start | bytes 7864320 | tf_op jit(solution)/shard_map/all_gather | solution.py:168
  109.9 23.9 copy-start.25
  128.4 610.5 %copy-start.32 = (bf16[2048,16]{0,1:T(8,128)(2,1)}, bf16[2048,16]{0,1:T(8,128)(2,1)S(1)}, u32[]{:S(2)}) copy-start(bf16[2048,16]{0,1:T(8,128)(2,1)S(1)} %all_gather.48) | copy-start | bytes 196612
  133.8 332.0 %copy-start.49 = (s32[1024]{0:T(1024)}, s32[1024]{0:T(1024)S(1)}, u32[]{:S(2)}) copy-start(s32[1024]{0:T(1024)S(1)} %fusion.88) | copy-start | bytes 12292
  465.8 9.6 copy-start.62
  508.1 229.6 %copy-start.7 = (bf16[4,1024,128]{2,1,0:T(8,128)(2,1)}, bf16[4,1024,128]{2,1,0:T(8,128)(2,1)S(1)}, u32[]{:S(2)}) copy-start(bf16[4,1024,128]{2,1,0:T(8,128)(2,1)S(1)} %get-tuple-element.572) | copy-start | bytes 3145732
  508.1 229.6 %copy-start.15 = (bf16[4,8,128,128]{3,2,1,0:T(8,128)(2,1)}, bf16[4,8,128,128]{3,2,1,0:T(8,128)(2,1)S(1)}, u32[]{:S(2)}) copy-start(bf16[4,8,128,128]{3,2,1,0:T(8,128)(2,1)S(1)} %get-tuple-element.573) | copy-start | bytes 3145732
  508.1 229.6 %copy-start.34 = (s32[1024]{0:T(1024)}, s32[1024]{0:T(1024)S(1)}, u32[]{:S(2)}) copy-start(s32[1024]{0:T(1024)S(1)} %get-tuple-element.614) | copy-start | bytes 12292
  508.1 229.6 %copy-start.39 = (s32[1024]{0:T(1024)}, s32[1024]{0:T(1024)S(1)}, u32[]{:S(2)}) copy-start(s32[1024]{0:T(1024)S(1)} %get-tuple-element.630) | copy-start | bytes 12292
  508.1 229.6 %copy-start.51 = (s32[128]{0:T(128)}, s32[128]{0:T(128)S(1)}, u32[]{:S(2)}) copy-start(s32[128]{0:T(128)S(1)} %get-tuple-element.634) | copy-start | bytes 1540
  729.1 9.6 copy-start.47
  738.9 24.4 copy-start.19
  739.2 8.0 copy-start.24
  757.8 76.3 %all-to-all-start.2 = ((bf16[8,2,96,2048]{3,2,1,0:T(8,128)(2,1)}), bf16[8,2,96,2048]{3,2,1,0:T(8,128)(2,1)}, u32[]{:S(2)}, u32[]{:S(2)}) async-start(bf16[8,2,96,2048]{3,2,1,0:T(8,128)(2,1)} %bitcast.323), calls=%async_computation.2 | async-start | bytes 12582912 | tf_op jit(solution)/shard_map/all_to_all | solution.py:215
  762.6 312.0 %all-gather.28.cloned.1.call-start = ((), (), s32[]{:S(2)}) async-start(), calls=%async_computation.22 | async-start | bytes 7864320 | tf_op jit(solution)/shard_map/all_gather | solution.py:169
  834.2 76.4 %all-to-all-start = ((bf16[8,2,96,2048]{3,2,1,0:T(8,128)(2,1)}), bf16[8,2,96,2048]{3,2,1,0:T(8,128)(2,1)}, u32[]{:S(2)}, u32[]{:S(2)}) async-start(bf16[8,2,96,2048]{3,2,1,0:T(8,128)(2,1)} %bitcast.324), calls=%async_computation | async-start | bytes 12582912 | tf_op jit(solution)/shard_map/all_to_all | solution.py:190
  1074.6 13.9 copy-start.66
  1114.2 76.8 %all-to-all-start.1 = ((bf16[1,2,768,2048]{3,1,0,2:T(2,128)(2,1)}), bf16[1,2,768,2048]{3,1,0,2:T(2,128)(2,1)}, u32[]{:S(2)}, u32[]{:S(2)}) async-start(bf16[1,2,768,2048]{3,1,0,2:T(2,128)(2,1)} %copy.93), calls=%async_computation.1 | async-start | bytes 12582912 | tf_op jit(solution)/shard_map/all_to_all | solution.py:203
  1119.4 10.7 copy-start.68
  1159.1 36.7 %copy-start.50 = (s32[1024]{0:T(1024)S(1)}, s32[1024]{0:T(1024)}, u32[]{:S(2)}) copy-start(s32[1024]{0:T(1024)} %copy-done.49) | copy-start | bytes 12292
  1190.9 76.3 %all-to-all-start.3 = ((bf16[1,2,768,2048]{3,1,0,2:T(2,128)(2,1)}), bf16[1,2,768,2048]{3,1,0,2:T(2,128)(2,1)}, u32[]{:S(2)}, u32[]{:S(2)}) async-start(bf16[1,2,768,2048]{3,1,0,2:T(2,128)(2,1)} %copy.96), calls=%async_computation.3 | async-start | bytes 12582912 | tf_op jit(solution)/shard_map/all_to_all | solution.py:230
  1195.7 213.7 %reduce-scatter.31.cloned.1.call-start = ((), (), s32[]{:S(2)}) async-start(), calls=%async_computation.32 | async-start | bytes 1179648
  1288.3 8.3 copy-start.27
  1298.3 153.5 %copy-start.9 = (f32[128,2048]{1,0:T(8,128)}, f32[128,2048]{1,0:T(8,128)S(1)}, u32[]{:S(2)}) copy-start(f32[128,2048]{1,0:T(8,128)S(1)} %get-tuple-element.290) | copy-start | bytes 3145732
  1374.5 36.0 %copy-start.29 = (f32[128,64]{0,1:T(8,128)S(1)}, f32[128,64]{0,1:T(8,128)}, u32[]{:S(2)}) copy-start(f32[128,64]{0,1:T(8,128)} %copy-done.28) | copy-start | bytes 98308
  1374.5 36.0 %copy-start.31 = (f32[128,64]{0,1:T(8,128)S(1)}, f32[128,64]{0,1:T(8,128)}, u32[]{:S(2)}) copy-start(f32[128,64]{0,1:T(8,128)} %copy-done.30) | copy-start | bytes 98308
  1374.5 36.0 %copy-start.23 = (f32[128,4,128]{0,2,1:T(8,128)S(1)}, f32[128,4,128]{0,2,1:T(8,128)}, u32[]{:S(2)}) copy-start(f32[128,4,128]{0,2,1:T(8,128)} %copy-done.22) | copy-start | bytes 786436
  1374.5 36.0 %copy-start.55 = (f32[128,4]{0,1:T(4,128)S(1)}, f32[128,4]{0,1:T(4,128)}, u32[]{:S(2)}) copy-start(f32[128,4]{0,1:T(4,128)} %copy-done.54) | copy-start | bytes 6148
  1374.5 36.0 %copy-start.61 = (f32[128]{0:T(128)S(1)}, f32[128]{0:T(128)}, u32[]{:S(2)}) copy-start(f32[128]{0:T(128)} %param.32) | copy-start | bytes 1540
  1374.5 36.3 %copy-start.14 = (bf16[1,128,2048]{2,1,0:T(8,128)(2,1)S(1)}, bf16[1,128,2048]{2,1,0:T(8,128)(2,1)}, u32[]{:S(2)}) copy-start(bf16[1,128,2048]{2,1,0:T(8,128)(2,1)} %copy-done.13) | copy-start | bytes 1572868
  1376.9 71.7 %reduce-scatter.33.cloned.1.call-start = ((), (), s32[]{:S(2)}) async-start(), calls=%async_computation.33 | async-start | bytes 1179648
  1379.2 69.3 %copy-start.4 = (f32[1,128,2048]{2,1,0:T(8,128)S(1)}, f32[1,128,2048]{2,1,0:T(8,128)}, u32[]{:S(2)}) copy-start(f32[1,128,2048]{2,1,0:T(8,128)} %param.23) | copy-start | bytes 3145732
  1379.2 69.3 %copy-start.46 = (f32[2048]{0:T(1024)S(1)}, f32[2048]{0:T(1024)}, u32[]{:S(2)}) copy-start(f32[2048]{0:T(1024)} %param.27) | copy-start | bytes 24580
  1379.2 69.3 %copy-start.59 = (f32[128]{0:T(128)S(1)}, f32[128]{0:T(128)}, u32[]{:S(2)}) copy-start(f32[128]{0:T(128)} %copy-done.58) | copy-start | bytes 1540
  1379.3 132.8 %reduce-scatter.17.cloned.1.call-start = ((), (), s32[]{:S(2)}) async-start(), calls=%async_computation.24 | async-start | bytes 2621440 | tf_op jit(solution)/shard_map/reduce_scatter | solution.py:324
  1412.9 126.6 %reduce-scatter.19.cloned.1.call-start = ((), (), s32[]{:S(2)}) async-start(), calls=%async_computation.25 | async-start | bytes 2621440 | tf_op jit(solution)/shard_map/reduce_scatter | solution.py:327
  1451.7 369.8 %reduce-scatter.21.cloned.1.call-start = ((), (), s32[]{:S(2)}) async-start(), calls=%async_computation.26 | async-start | bytes 20971520 | tf_op jit(solution)/shard_map/reduce_scatter | solution.py:330
  1461.1 643.6 %reduce-scatter.15.cloned.1.call-start = ((), (), s32[]{:S(2)}) async-start(), calls=%async_computation.23 | async-start | bytes 20971520 | tf_op jit(solution)/shard_map/reduce_scatter | solution.py:321
  1480.5 646.8 %reduce-scatter.23.cloned.1.call-start = ((), (), s32[]{:S(2)}) async-start(), calls=%async_computation.27 | async-start | bytes 81920 | tf_op jit(solution)/shard_map/reduce_scatter | solution.py:333
  1482.5 757.0 %reduce-scatter.29.cloned.1.call-start = ((), (), s32[]{:S(2)}) async-start(), calls=%async_computation.30 | async-start | bytes 7864320 | tf_op jit(solution)/shard_map/reduce_scatter | solution.py:316
  1492.2 861.3 %reduce-scatter.25.cloned.1.call-start = ((), (), s32[]{:S(2)}) async-start(), calls=%async_computation.28 | async-start | bytes 7864320 | tf_op jit(solution)/shard_map/reduce_scatter | solution.py:310
  1502.0 965.1 %reduce-scatter.27.cloned.1.call-start = ((), (), s32[]{:S(2)}) async-start(), calls=%async_computation.29 | async-start | bytes 7864320 | tf_op jit(solution)/shard_map/reduce_scatter | solution.py:313
  1511.9 1051.5 %all-reduce.4.cloned.1.call-start = ((), (), s32[]{:S(2)}) async-start(), calls=%async_computation.34 | async-start | bytes 10485760 | tf_op jit(solution)/shard_map/psum | solution.py:341
  1821.4 283.3 %copy-start.17 = (bf16[128,32,128]{0,2,1:T(8,128)(2,1)S(1)}, bf16[128,32,128]{0,2,1:T(8,128)(2,1)}, u32[]{:S(2)}) copy-start(bf16[128,32,128]{0,2,1:T(8,128)(2,1)} %multiply_convert_fusion.4) | copy-start | bytes 3145732
  1821.5 904.7 %all-gather.30.cloned.1.call-start = ((), (), s32[]{:S(2)}) async-start(), calls=%async_computation.31 | async-start | bytes 37748736 | tf_op jit(solution)/shard_map/all_gather | solution.py:338
  2116.3 38.0 %copy-start.38 = (bf16[128,512]{1,0:T(8,128)(2,1)S(1)}, bf16[128,512]{1,0:T(8,128)(2,1)}, u32[]{:S(2)}) copy-start(bf16[128,512]{1,0:T(8,128)(2,1)} %reduce-scatter.33.cloned.1.call-done) | copy-start | bytes 393220
  2151.7 46.2 %copy-start.10 = (f32[128,2048]{1,0:T(8,128)S(1)}, f32[128,2048]{1,0:T(8,128)}, u32[]{:S(2)}) copy-start(f32[128,2048]{1,0:T(8,128)} %copy-done.9) | copy-start | bytes 3145732
  2726.2 20.9 copy-start.1
  (33 other events, 133.1 us)
Sparse Core Ops, SparseCore 0:
  9.6 48.3 all-gather.13
  59.6 44.4 all-gather.17
  106.5 22.2 all-gather.15
  131.1 23.3 all-gather.19
  156.0 286.7 all-gather.11
  444.2 284.9 all-gather.21
  730.7 113.5 all-gather.23
  845.8 113.5 all-gather.25
  961.0 113.5 all-gather.27
  1377.0 32.3 reduce-scatter.30
  1412.6 35.9 reduce-scatter.32
  1450.7 43.6 reduce-scatter.16
  1496.7 42.8 reduce-scatter.18
  1541.7 279.6 reduce-scatter.20
  1823.6 281.0 reduce-scatter.14
  2107.4 19.9 reduce-scatter.22
  2129.5 109.9 reduce-scatter.28
  2242.2 111.2 reduce-scatter.24
  2355.8 111.2 reduce-scatter.26
  2470.5 92.9 all-reduce.3
  2565.4 160.7 all-gather.29
